TPU v7x, 256 devices: a whole 4x4x8 slice. The times are simulated.
256 devices in a mesh: section: 16 (over y, x), dp: 16 (over z, core).
Axes of the slice: x: 4, y: 4, z: 8, core: 2. Of those that a mesh axis runs over, the one named last changes fastest.
Arguments:
- hidden: bfloat16 [16, 256, 8192], P('dp', 'section'), may hold values from -1500 to 1500
- head: bfloat16 [65536, 8192], P('section', 'dp'), may hold values from -0.0625 to 0.0625
- block_id: int32 [16, 16], P(None, 'section'), may hold values from 0 to 7
- block_live: int32 [16, 16], P(None, 'section'), may hold values from 0 to 1, as said below
- teacher: bfloat16 [16, 256, 8192], P('dp', None, 'section'), may hold values from -400 to 400
Outputs:
- grad_hidden: bfloat16 [16, 256, 8192], P('dp', 'section')
- grad_head: bfloat16 [65536, 8192], P('section', 'dp')
Inputs may be any that keep to these rules, and one draw needn't show every extreme that they name: `block_live`: every micro-batch has at least one live section.
All inputs are finite; a program needn't handle non-finite values.
Results may differ from a plain program's by a relative error of at most 0.0056.
Values may be sent and summed in bfloat16 or wider, within the bound.
No kernel may reach another device: no remote copies, remote signals or barrier semaphores. Data moves between devices by JAX's collectives and lax.ppermute only.
A program may use at most 128 MiB of HBM per device.

v0:
```python
import jax
import jax.numpy as jnp
from jax import lax
from jax.sharding import PartitionSpec as P

neg_fill = -1e30


def local(hidden, head, block_id, block_live, teacher):
    my_replica = lax.axis_index("dp")
    tok_local = hidden.shape[1]
    model_width = hidden.shape[2]
    block_rows = teacher.shape[2]
    col_width = head.shape[1]
    blocks = head.shape[0] // block_rows
    table = head.reshape(blocks, block_rows, col_width)
    block_ids = block_id[:, 0]
    live_flags = block_live[:, 0]
    picked = jnp.take(table, block_ids, axis=0)
    whole = lax.all_gather(hidden, "section", axis=1, tiled=True)
    hidden_rows = whole[0]
    own_live = lax.dynamic_index_in_dim(live_flags, my_replica, 0, keepdims=False) > 0
    full_rows = lax.all_to_all(picked, "dp", split_axis=0, concat_axis=2, tiled=True)[0]
    logits = jnp.einsum("td,rd->tr", hidden_rows, full_rows, preferred_element_type=jnp.float32)
    teach = teacher[0].astype(jnp.float32)
    live_value = jnp.where(own_live, 1.0, 0.0).astype(jnp.float32)
    stud_local = jnp.where(own_live, jnp.max(logits, axis=1), neg_fill)
    teach_local = jnp.where(own_live, jnp.max(teach, axis=1), neg_fill)
    stud_top, teach_top = lax.pmax((stud_local, teach_local), "section")
    stud_part = jnp.where(own_live, jnp.sum(jnp.exp(logits - stud_top[:, None]), axis=1), 0.0)
    teach_part = jnp.where(own_live, jnp.sum(jnp.exp(teach - teach_top[:, None]), axis=1), 0.0)
    stud_total, teach_total, live_count = lax.psum((stud_part, teach_part, live_value), "section")
    student = jnp.where(own_live, jnp.exp(logits - stud_top[:, None]) / stud_total[:, None], 0.0)
    teach_prob = jnp.where(
        own_live, jnp.exp(teach - teach_top[:, None]) / teach_total[:, None], 0.0
    )
    logit_grad = (block_rows * live_count * (student - teach_prob)).astype(jnp.bfloat16)
    summed = lax.psum_scatter(
        jnp.dot(logit_grad, full_rows, preferred_element_type=jnp.float32),
        "section",
        scatter_dimension=0,
        tiled=True,
    )
    grad_hidden = summed.astype(jnp.bfloat16).reshape(1, tok_local, model_width)
    contrib = jnp.einsum(
        "tr,td->rd", logit_grad, hidden_rows, preferred_element_type=jnp.float32
    ).astype(jnp.bfloat16)
    returned = lax.all_to_all(contrib[None], "dp", split_axis=2, concat_axis=0, tiled=True)
    block_range = jnp.arange(blocks, dtype=jnp.int32)[None, :]
    selector = jnp.where(
        (live_flags[:, None] > 0) & (block_ids[:, None] == block_range), 1.0, 0.0
    ).astype(jnp.bfloat16)
    grad_head = jnp.einsum("mb,mrc->brc", selector, returned, preferred_element_type=jnp.float32)
    grad_head = grad_head.astype(jnp.bfloat16).reshape(blocks * block_rows, col_width)
    return (grad_hidden, grad_head)


def solution(mesh):
    placed = (
        P("dp", "section", None),
        P("section", "dp"),
        P(None, "section"),
        P(None, "section"),
        P("dp", None, "section"),
    )
    return jax.shard_map(
        local,
        mesh=mesh,
        in_specs=placed,
        out_specs=(P("dp", "section", None), P("section", "dp")),
        check_vma=False,
    )
```

profile of v0, /device:TPU:1, one launch (start us, length us, event | category | flops | bytes accessed | tf_op | source)
XLA Modules:
  0.0 687.1 jit_solution(2337014340000765486)
XLA Ops:
  7.2 0.7 fusion.26
  7.8 0.7 and_bitcast_fusion
  8.5 7.0 %gather_fusion = bf16[16,512,512]{2,1,0:T(8,128)(2,1)} fusion(bf16[8,512,512]{2,1,0:T(8,128)(2,1)} %bitcast.57, s32[1024]{0:T(1024)S(1)} %pad_clamp_fusion), kind=kCustom, calls=%fused_computation | custom fusion | bytes 16777280 | tf_op jit(solution)/shard_map/jit(_take)/gather | solution.py:19
  15.4 7.5 %broadcast_select_fusion = bf16[16,512,512]{2,1,0:T(8,128)(2,1)} fusion(bf16[16,512,512]{2,1,0:T(8,128)(2,1)} %gather_fusion, pred[16]{0:T(512)(128)(4,1)S(1)} %and_bitcast_fusion), kind=kLoop, calls=%fused_computation.5 | loop fusion | flops 4194304 | bytes 16777232 | tf_op jit(solution)/shard_map/jit(_take)/select_n | solution.py:19
  22.9 10.1 %all-to-all-start = ((bf16[16,512,512]{2,1,0:T(8,128)(2,1)}), bf16[16,512,512]{2,1,0:T(8,128)(2,1)}, u32[]{:S(2)}, u32[]{:S(2)}) async-start(bf16[16,512,512]{2,1,0:T(8,128)(2,1)} %broadcast_select_fusion), calls=%async_computation | async-start | bytes 16777216 | tf_op jit(solution)/shard_map/all_to_all | solution.py:23
  33.1 0.7 all-gather.2.cloned.1.call-update
  35.3 181.2 %all-to-all-done = bf16[16,512,512]{2,1,0:T(8,128)(2,1)} async-done(((bf16[16,512,512]{2,1,0:T(8,128)(2,1)}), bf16[16,512,512]{2,1,0:T(8,128)(2,1)}, u32[]{:S(2)}, u32[]{:S(2)}) %all-to-all-start) | async-done | bytes 8388640 | tf_op jit(solution)/shard_map/all_to_all | solution.py:23
  216.6 12.3 %copy.13 = bf16[1,512,16,512]{1,3,2,0:T(8,128)(2,1)} copy(bf16[1,512,16,512]{3,1,2,0:T(8,128)(2,1)} %bitcast.5) | data formatting | bytes 16777216 | tf_op jit(solution)/shard_map/all_to_all | solution.py:23
  228.9 7.0 %fusion.31 = (f32[256]{0:T(256)S(1)}, f32[512,256]{1,0:T(8,128)S(1)}) fusion(bf16[512,8192]{0,1:T(8,128)(2,1)} %bitcast.55, bf16[1,256,8192]{2,1,0:T(8,128)(2,1)} %all-gather.2.cloned.1.call-done), kind=kOutput, calls=%fused_computation.43 | convolution fusion | flops 2147614464 | bytes 13108224 | tf_op jit(solution)/shard_map/td,rd->tr/dot_general | solution.py:24
  236.5 33.4 %all-reduce.1 = (f32[256]{0:T(256)S(1)}, f32[256]{0:T(256)S(1)}) all-reduce(f32[256]{0:T(256)S(1)} %get-tuple-element.9, f32[256]{0:T(256)S(1)} %get-tuple-element.10), channel_id=1, replica_groups=mesh['section'=16,'dp'=16] {'section'}, use_global_device_ids=true, to_apply=%region_6.7 | all-reduce | flops 512 | bytes 4096 | tf_op jit(solution)/shard_map/pmax | solution.py:29
  271.5 29.2 %all-reduce = (f32[256]{0:T(256)S(1)}, f32[256]{0:T(256)S(1)}, f32[]{:T(128)}) all-reduce(f32[256]{0:T(256)S(1)} %broadcast_select_fusion.1, f32[256]{0:T(256)S(1)} %broadcast_select_fusion.2, f32[]{:T(128)S(6)} %select_n.61), channel_id=1, replica_groups=mesh['section'=16,'dp'=16] {'section'}, use_global_device_ids=true, to_apply=%region_8.9 | all-reduce | flops 513 | bytes 4104 | tf_op jit(solution)/shard_map/psum | solution.py:32
  301.3 9.8 %fusion.28 = f32[256,8192]{1,0:T(8,128)} fusion(bf16[512,8192]{0,1:T(8,128)(2,1)} %bitcast.56, f32[512,256]{1,0:T(8,128)S(1)} %get-tuple-element.8, bf16[1,256,512]{1,2,0:T(8,128)(2,1)S(1)} %copy.14, f32[256]{0:T(256)S(1)} %get-tuple-element.2, f32[256]{0:T(256)S(1)} %get-tuple-element.5, f32[256]{0:T(256)S(1)} %get-tuple-element.3, ...), kind=kOutput, calls=%fused_computation.41 | convolution fusion | flops 2148794368 | bytes 17567748 | tf_op jit(solution)/shard_map/dot_general | solution.py:39
  311.2 8.5 %fusion = bf16[1,512,8192]{2,1,0:T(8,128)(2,1)} fusion(bf16[1,256,8192]{2,1,0:T(8,128)(2,1)} %all-gather.2.cloned.1.call-done, f32[512,256]{1,0:T(8,128)S(1)} %get-tuple-element.8, bf16[1,256,512]{1,2,0:T(8,128)(2,1)S(1)} %copy.14, f32[256]{0:T(256)S(1)} %get-tuple-element.2, f32[256]{0:T(256)S(1)} %get-tuple-element.5, f32[256]{0:T(256)S(1)} %get-tuple-element.3, ...), kind=kOutput, calls=%fused_computation.2 | convolution fusion | flops 2152988672 | bytes 13373445 | tf_op jit(solution)/shard_map/tr,td->rd/dot_general | solution.py:45
  319.7 34.7 %copy.15 = bf16[1,512,8192]{1,0,2:T(2,128)(2,1)} copy(bf16[1,512,8192]{2,1,0:T(8,128)(2,1)} %fusion) | data formatting | bytes 16777216 | tf_op jit(solution)/shard_map/broadcast_in_dim | solution.py:48
  355.0 54.7 %reduce.4 = bf16[8192,512]{1,0:T(8,128)(2,1)} reduce(bf16[8192,1,512]{2,1,0:T(2,128)(2,1)} %bitcast.53, bf16[]{:T(256)} %broadcast.31), dimensions={1}, to_apply=%bitcast.46.reduce_sub_computation | reduce | bytes 16777218
  409.6 14.6 %reshape.42 = bf16[16,2,131072]{2,1,0:T(2,128)(2,1)} reshape(bf16[8192,512]{1,0:T(8,128)(2,1)} %reduce.4) | data formatting | bytes 16777216
  424.3 19.7 %all-to-all-start.1 = ((bf16[16,2,131072]{2,1,0:T(2,128)(2,1)}), bf16[16,2,131072]{2,1,0:T(2,128)(2,1)}, u32[]{:S(2)}, u32[]{:S(2)}) async-start(bf16[16,2,131072]{2,1,0:T(2,128)(2,1)} %reshape.42), calls=%async_computation.2 | async-start | bytes 16777216 | tf_op jit(solution)/shard_map/all_to_all | solution.py:48
  443.9 183.5 %all-to-all-done.1 = bf16[16,2,131072]{2,1,0:T(2,128)(2,1)} async-done(((bf16[16,2,131072]{2,1,0:T(2,128)(2,1)}), bf16[16,2,131072]{2,1,0:T(2,128)(2,1)}, u32[]{:S(2)}, u32[]{:S(2)}) %all-to-all-start.1) | async-done | bytes 8388640 | tf_op jit(solution)/shard_map/all_to_all | solution.py:48
  627.4 16.5 %reshape.43 = bf16[8192,1,512]{2,1,0:T(2,128)(2,1)} reshape(bf16[16,2,131072]{2,1,0:T(2,128)(2,1)} %all-to-all-done.1) | data formatting | bytes 16777216
  643.9 11.6 %copy.19 = bf16[1,512,8192]{1,2,0:T(8,128)(2,1)} copy(bf16[1,512,8192]{1,0,2:T(2,128)(2,1)} %bitcast.52) | data formatting | bytes 16777216
  655.5 14.9 %copy.18 = bf16[1,512,16,512]{3,2,1,0:T(8,128)(2,1)} copy(bf16[1,512,16,512]{1,3,2,0:T(8,128)(2,1)} %bitcast.54) | data formatting | bytes 16777216 | tf_op jit(solution)/shard_map/all_to_all | solution.py:48
  670.4 4.6 fusion.6
  675.1 3.5 copy.17
  678.5 1.8 convert_bitcast_fusion
  (22 shorter events, 3.7 us)
Async XLA Ops:
  22.9 10.9 %copy-start = (bf16[1,256,512]{2,1,0:T(8,128)(2,1)S(1)}, bf16[1,256,512]{2,1,0:T(8,128)(2,1)}, u32[]{:S(2)}) copy-start(bf16[1,256,512]{2,1,0:T(8,128)(2,1)} %param.9) | copy-start | bytes 786436
  22.9 11.2 %copy-start.2 = (s32[16,1]{0,1:T(1,128)S(1)}, s32[16,1]{0,1:T(1,128)}, u32[]{:S(2)}) copy-start(s32[16,1]{0,1:T(1,128)} %param.8) | copy-start | bytes 196
  22.9 193.6 %all-to-all-start = ((bf16[16,512,512]{2,1,0:T(8,128)(2,1)}), bf16[16,512,512]{2,1,0:T(8,128)(2,1)}, u32[]{:S(2)}, u32[]{:S(2)}) async-start(bf16[16,512,512]{2,1,0:T(8,128)(2,1)} %broadcast_select_fusion), calls=%async_computation | async-start | bytes 16777216 | tf_op jit(solution)/shard_map/all_to_all | solution.py:23
  33.0 195.8 %all-gather.2.cloned.1.call-start = ((), (), s32[]{:S(2)}) async-start(), calls=%async_computation.3 | async-start | bytes 4456448 | tf_op jit(solution)/shard_map/all_gather | solution.py:20
  33.8 644.8 %reduce-scatter.2.cloned.1.call-start = ((), (), s32[]{:S(2)}) async-start(), calls=%async_computation.4 | async-start | bytes 8912896 | tf_op jit(solution)/shard_map/reduce_scatter | solution.py:38
  424.3 203.1 %all-to-all-start.1 = ((bf16[16,2,131072]{2,1,0:T(2,128)(2,1)}), bf16[16,2,131072]{2,1,0:T(2,128)(2,1)}, u32[]{:S(2)}, u32[]{:S(2)}) async-start(bf16[16,2,131072]{2,1,0:T(2,128)(2,1)} %reshape.42), calls=%async_computation.2 | async-start | bytes 16777216 | tf_op jit(solution)/shard_map/all_to_all | solution.py:48
  655.5 14.9 %copy-start.1 = (s32[16,1]{0,1:T(1,128)S(1)}, s32[16,1]{0,1:T(1,128)}, u32[]{:S(2)}) copy-start(s32[16,1]{0,1:T(1,128)} %param.7) | copy-start | bytes 196
Sparse Core Ops, SparseCore 0:
  36.3 57.5 all-gather.1
  311.3 98.5 reduce-scatter.1
where the time goes:
time: 690 us; the launch traced here: 687 us
  waiting for transfers between devices  365 us (53%)
  local copies, waits for them, and re-layouts  116 us (17%)
  other arithmetic  68.1 us (10%)
  blocking collectives  62.6 us (9%)
  matrix products  30 us (4%)
  starting transfers between devices  29.8 us (4%)
  between operations  15.4 us (2%)
    all_to_all x1, waiting for transfers between devices, local(): lax.all_to_all(contrib[None], 'dp', split_axis=2, concat_axis=0, tiled=True)  183 us
    all_to_all x1, waiting for transfers between devices, local(): lax.all_to_all(picked, 'dp', split_axis=0, concat_axis=2, tiled=True)[0]  181 us
    unnamed x1, other arithmetic  54.7 us
    unnamed x11, local copies, waits for them, and re-layouts  43.4 us
    broadcast_in_dim x1, local copies, waits for them, and re-layouts, local(): contrib[None]  34.7 us
    pmax x1, blocking collectives, local(): stud_top, teach_top = lax.pmax((stud_local, teach_local), 'section')  33.4 us
    psum x1, blocking collectives, local(): lax.psum((stud_part, teach_part, live_value), 'section')  29.2 us
    all_to_all x1, starting transfers between devices, local(): lax.all_to_all(contrib[None], 'dp', split_axis=2, concat_axis=0, tiled=True)  19.7 us
  transfers between devices with their start and end apart: 4, of which 2 were waited for; matrix products, arithmetic and copies ran while one was open for 26% of the time, Pallas kernels for 0%

commit v1 on v0

--- a/solution.py
+++ b/solution.py
@@ -4,6 +4,16 @@
 from jax.sharding import PartitionSpec as P
 
 neg_fill = -1e30
+
+
+def _finish_kinds(values, device_axis):
+    latest = jnp.concatenate(
+        lax.all_to_all(
+            jnp.stack(jnp.split(values, lax.axis_size(device_axis), axis=0)), device_axis, 0, 0
+        ),
+        axis=2,
+    )
+    return latest
 
 
 def local(hidden, head, block_id, block_live, teacher):
@@ -20,7 +30,7 @@
     whole = lax.all_gather(hidden, "section", axis=1, tiled=True)
     hidden_rows = whole[0]
     own_live = lax.dynamic_index_in_dim(live_flags, my_replica, 0, keepdims=False) > 0
-    full_rows = lax.all_to_all(picked, "dp", split_axis=0, concat_axis=2, tiled=True)[0]
+    full_rows = _finish_kinds(picked, "dp")[0]
     logits = jnp.einsum("td,rd->tr", hidden_rows, full_rows, preferred_element_type=jnp.float32)
     teach = teacher[0].astype(jnp.float32)
     live_value = jnp.where(own_live, 1.0, 0.0).astype(jnp.float32)

time: 690 us -> 721 us (1.045)
  local copies, waits for them, and re-layouts: 116 us -> 146 us
    unnamed x11 -> x26, local copies, waits for them, and re-layouts: 43.4 us -> 71.6 us
    all_to_all x1 -> x0, local copies, waits for them, and re-layouts: 12.3 us -> none  [local(): lax.all_to_all(picked, 'dp', split_axis=0, concat_axis=2, tiled=True)[0]]
    reshape x0 -> x1, local copies, waits for them, and re-layouts: none -> 12.3 us  [_finish_kinds(): jnp.concatenate(lax.all_to_all(jnp.stack(jnp.split(values, lax.axis_size(...]
  transfers between devices with their start and end apart: 4 -> 4, of which waited for: 2 -> 2; matrix products, arithmetic and copies ran while one was open for 26% -> 25% of each run, Pallas kernels for 0% -> 0%
where the time goes in v1:
time: 721 us; the launch traced here: 717 us
  waiting for transfers between devices  365 us (51%)
  local copies, waits for them, and re-layouts  146 us (20%)
  other arithmetic  68.1 us (9%)
  blocking collectives  62.6 us (9%)
  matrix products  29.9 us (4%)
  starting transfers between devices  29.8 us (4%)
  between operations  15.4 us (2%)
    all_to_all x1, waiting for transfers between devices, local(): lax.all_to_all(contrib[None], 'dp', split_axis=2, concat_axis=0, tiled=True)  183 us
    all_to_all x1, waiting for transfers between devices, _finish_kinds(): lax.all_to_all(jnp.stack(jnp.split(values, lax.axis_size(device_axis), ax...  181 us
    unnamed x26, local copies, waits for them, and re-layouts  71.6 us
    unnamed x1, other arithmetic  54.7 us
    broadcast_in_dim x1, local copies, waits for them, and re-layouts, local(): contrib[None]  34.7 us
    pmax x1, blocking collectives, local(): stud_top, teach_top = lax.pmax((stud_local, teach_local), 'section')  33.4 us
    psum x1, blocking collectives, local(): lax.psum((stud_part, teach_part, live_value), 'section')  29.2 us
    all_to_all x1, starting transfers between devices, local(): lax.all_to_all(contrib[None], 'dp', split_axis=2, concat_axis=0, tiled=True)  19.7 us
  transfers between devices with their start and end apart: 4, of which 2 were waited for; matrix products, arithmetic and copies ran while one was open for 25% of the time, Pallas kernels for 0%

profile of v1, /device:TPU:1, one launch (start us, length us, event | category | flops | bytes accessed | tf_op | source)
XLA Modules:
  0.0 717.2 jit_solution(5863932435049776504)
XLA Ops:
  8.5 6.9 gather_fusion
  15.4 7.5 %broadcast_select_fusion = bf16[16,512,512]{2,1,0:T(8,128)(2,1)} fusion(bf16[16,512,512]{2,1,0:T(8,128)(2,1)} %gather_fusion, pred[16]{0:T(512)(128)(4,1)S(1)} %and_bitcast_fusion), kind=kLoop, calls=%fused_computation.5 | loop fusion | flops 4194304 | bytes 16777232 | tf_op jit(solution)/shard_map/jit(_take)/select_n | solution.py:29
  26.6 1.9 fusion.22
  36.0 1.9 fusion.17
  39.8 1.9 fusion.15
  47.3 1.9 fusion.11
  53.0 10.1 %all-to-all-start = ((bf16[16,1,512,512]{3,2,1,0:T(8,128)(2,1)}), bf16[16,1,512,512]{3,2,1,0:T(8,128)(2,1)}, u32[]{:S(2)}, u32[]{:S(2)}) async-start(bf16[16,1,512,512]{3,2,1,0:T(8,128)(2,1)} %fusion.9), calls=%async_computation | async-start | bytes 16777216 | tf_op jit(solution)/shard_map/all_to_all | solution.py:11
  65.4 181.2 %all-to-all-done = bf16[16,1,512,512]{3,2,1,0:T(8,128)(2,1)} async-done(((bf16[16,1,512,512]{3,2,1,0:T(8,128)(2,1)}), bf16[16,1,512,512]{3,2,1,0:T(8,128)(2,1)}, u32[]{:S(2)}, u32[]{:S(2)}) %all-to-all-start) | async-done | bytes 8388640 | tf_op jit(solution)/shard_map/all_to_all | solution.py:11
  246.6 12.3 %copy.28 = bf16[1,512,16,512]{1,3,2,0:T(8,128)(2,1)} copy(bf16[1,512,16,512]{3,1,0,2:T(8,128)(2,1)} %bitcast.20) | data formatting | bytes 16777216 | tf_op jit(solution)/shard_map/reshape | solution.py:10
  258.9 7.0 fusion.47
  266.6 33.4 %all-reduce.1 = (f32[256]{0:T(256)S(1)}, f32[256]{0:T(256)S(1)}) all-reduce(f32[256]{0:T(256)S(1)} %get-tuple-element.9, f32[256]{0:T(256)S(1)} %get-tuple-element.10), channel_id=1, replica_groups=mesh['section'=16,'dp'=16] {'section'}, use_global_device_ids=true, to_apply=%region_6.7 | all-reduce | flops 512 | bytes 4096 | tf_op jit(solution)/shard_map/pmax | solution.py:39
  301.6 29.2 %all-reduce = (f32[256]{0:T(256)S(1)}, f32[256]{0:T(256)S(1)}, f32[]{:T(128)}) all-reduce(f32[256]{0:T(256)S(1)} %broadcast_select_fusion.1, f32[256]{0:T(256)S(1)} %broadcast_select_fusion.2, f32[]{:T(128)S(6)} %select_n.61), channel_id=1, replica_groups=mesh['section'=16,'dp'=16] {'section'}, use_global_device_ids=true, to_apply=%region_8.9 | all-reduce | flops 513 | bytes 4104 | tf_op jit(solution)/shard_map/psum | solution.py:42
  331.4 9.8 %fusion.44 = f32[256,8192]{1,0:T(8,128)} fusion(bf16[512,8192]{0,1:T(8,128)(2,1)} %bitcast.118, f32[512,256]{1,0:T(8,128)S(1)} %get-tuple-element.8, bf16[1,256,512]{1,2,0:T(8,128)(2,1)S(1)} %copy.29, f32[256]{0:T(256)S(1)} %get-tuple-element.2, f32[256]{0:T(256)S(1)} %get-tuple-element.5, f32[256]{0:T(256)S(1)} %get-tuple-element.3, ...), kind=kOutput, calls=%fused_computation.73 | convolution fusion | flops 2148794368 | bytes 17567748 | tf_op jit(solution)/shard_map/dot_general | solution.py:49
  341.3 8.5 %fusion = bf16[1,512,8192]{2,1,0:T(8,128)(2,1)} fusion(bf16[1,256,8192]{2,1,0:T(8,128)(2,1)} %all-gather.2.cloned.1.call-done, f32[512,256]{1,0:T(8,128)S(1)} %get-tuple-element.8, bf16[1,256,512]{1,2,0:T(8,128)(2,1)S(1)} %copy.29, f32[256]{0:T(256)S(1)} %get-tuple-element.2, f32[256]{0:T(256)S(1)} %get-tuple-element.5, f32[256]{0:T(256)S(1)} %get-tuple-element.3, ...), kind=kOutput, calls=%fused_computation.2 | convolution fusion | flops 2152988672 | bytes 13373445 | tf_op jit(solution)/shard_map/tr,td->rd/dot_general | solution.py:55
  349.8 34.7 %copy.30 = bf16[1,512,8192]{1,0,2:T(2,128)(2,1)} copy(bf16[1,512,8192]{2,1,0:T(8,128)(2,1)} %fusion) | data formatting | bytes 16777216 | tf_op jit(solution)/shard_map/broadcast_in_dim | solution.py:58
  385.1 54.7 %reduce.4 = bf16[8192,512]{1,0:T(8,128)(2,1)} reduce(bf16[8192,1,512]{2,1,0:T(2,128)(2,1)} %bitcast.115, bf16[]{:T(256)} %broadcast.31), dimensions={1}, to_apply=%bitcast.108.reduce_sub_computation | reduce | bytes 16777218
  439.7 14.6 %reshape.45 = bf16[16,2,131072]{2,1,0:T(2,128)(2,1)} reshape(bf16[8192,512]{1,0:T(8,128)(2,1)} %reduce.4) | data formatting | bytes 16777216
  454.3 19.7 %all-to-all-start.1 = ((bf16[16,2,131072]{2,1,0:T(2,128)(2,1)}), bf16[16,2,131072]{2,1,0:T(2,128)(2,1)}, u32[]{:S(2)}, u32[]{:S(2)}) async-start(bf16[16,2,131072]{2,1,0:T(2,128)(2,1)} %reshape.45), calls=%async_computation.2 | async-start | bytes 16777216 | tf_op jit(solution)/shard_map/all_to_all | solution.py:58
  474.0 183.5 %all-to-all-done.1 = bf16[16,2,131072]{2,1,0:T(2,128)(2,1)} async-done(((bf16[16,2,131072]{2,1,0:T(2,128)(2,1)}), bf16[16,2,131072]{2,1,0:T(2,128)(2,1)}, u32[]{:S(2)}, u32[]{:S(2)}) %all-to-all-start.1) | async-done | bytes 8388640 | tf_op jit(solution)/shard_map/all_to_all | solution.py:58
  657.5 16.5 %reshape.46 = bf16[8192,1,512]{2,1,0:T(2,128)(2,1)} reshape(bf16[16,2,131072]{2,1,0:T(2,128)(2,1)} %all-to-all-done.1) | data formatting | bytes 16777216
  674.0 11.6 %copy.34 = bf16[1,512,8192]{1,2,0:T(8,128)(2,1)} copy(bf16[1,512,8192]{1,0,2:T(2,128)(2,1)} %bitcast.114) | data formatting | bytes 16777216
  685.6 14.9 %copy.33 = bf16[1,512,16,512]{3,2,1,0:T(8,128)(2,1)} copy(bf16[1,512,16,512]{1,3,2,0:T(8,128)(2,1)} %bitcast.116) | data formatting | bytes 16777216 | tf_op jit(solution)/shard_map/all_to_all | solution.py:58
  700.5 4.6 fusion.6
  705.1 3.5 copy.32
  (38 shorter events, 30.0 us)
Async XLA Ops:
  53.0 10.9 %copy-start = (bf16[1,256,512]{2,1,0:T(8,128)(2,1)S(1)}, bf16[1,256,512]{2,1,0:T(8,128)(2,1)}, u32[]{:S(2)}) copy-start(bf16[1,256,512]{2,1,0:T(8,128)(2,1)} %param.9) | copy-start | bytes 786436
  53.0 11.2 %copy-start.2 = (s32[16,1]{0,1:T(1,128)S(1)}, s32[16,1]{0,1:T(1,128)}, u32[]{:S(2)}) copy-start(s32[16,1]{0,1:T(1,128)} %param.8) | copy-start | bytes 196
  53.0 193.6 %all-to-all-start = ((bf16[16,1,512,512]{3,2,1,0:T(8,128)(2,1)}), bf16[16,1,512,512]{3,2,1,0:T(8,128)(2,1)}, u32[]{:S(2)}, u32[]{:S(2)}) async-start(bf16[16,1,512,512]{3,2,1,0:T(8,128)(2,1)} %fusion.9), calls=%async_computation | async-start | bytes 16777216 | tf_op jit(solution)/shard_map/all_to_all | solution.py:11
  63.1 195.8 %all-gather.2.cloned.1.call-start = ((), (), s32[]{:S(2)}) async-start(), calls=%async_computation.3 | async-start | bytes 4456448 | tf_op jit(solution)/shard_map/all_gather | solution.py:30
  63.8 644.8 %reduce-scatter.2.cloned.1.call-start = ((), (), s32[]{:S(2)}) async-start(), calls=%async_computation.4 | async-start | bytes 8912896 | tf_op jit(solution)/shard_map/reduce_scatter | solution.py:48
  454.3 203.1 %all-to-all-start.1 = ((bf16[16,2,131072]{2,1,0:T(2,128)(2,1)}), bf16[16,2,131072]{2,1,0:T(2,128)(2,1)}, u32[]{:S(2)}, u32[]{:S(2)}) async-start(bf16[16,2,131072]{2,1,0:T(2,128)(2,1)} %reshape.45), calls=%async_computation.2 | async-start | bytes 16777216 | tf_op jit(solution)/shard_map/all_to_all | solution.py:58
  685.6 14.9 %copy-start.1 = (s32[16,1]{0,1:T(1,128)S(1)}, s32[16,1]{0,1:T(1,128)}, u32[]{:S(2)}) copy-start(s32[16,1]{0,1:T(1,128)} %param.7) | copy-start | bytes 196
Sparse Core Ops, SparseCore 0:
  66.4 57.5 all-gather.1
  341.4 98.5 reduce-scatter.1
